TPU v7x, 32 devices: a whole 2x2x4 slice. The times are simulated.
32 devices in a mesh: seq: 4 (over y, x), tp: 8 (over z, core).
Axes of the slice: x: 2, y: 2, z: 4, core: 2. Of those that a mesh axis runs over, the one named last changes fastest.
Arguments:
- streams: bfloat16 [3, 4096, 1024], P(None, 'tp', 'seq'), may hold values from -6 to 6
- feat_weight: float32 [3, 4096, 7], P(None, 'tp'), may hold values from -2 to 2
- long_filter: float32 [4096, 128], P('tp'), may hold values from -0.5 to 0.5
- skip_gain: float32 [4096], P('tp'), may hold values from -1 to 1
- out_weight: bfloat16 [4096, 4096], P('tp', 'seq'), may hold values from -0.125 to 0.125
- out_grad: bfloat16 [4096, 1024], P('tp', 'seq'), may hold values from -6 to 6
Outputs:
- mixed: bfloat16 [4096, 1024], P('tp', 'seq')
- stream_grad: bfloat16 [3, 4096, 1024], P(None, 'tp', 'seq')
- weight_grad: bfloat16 [4096, 4096], P('tp', 'seq')
All inputs are finite; a program needn't handle non-finite values.
Results may differ from a plain program's by a relative error of at most 0.009.
Values may be sent and summed in bfloat16 or wider, within the bound.
No kernel may reach another device: no remote copies, remote signals or barrier semaphores. Data moves between devices by JAX's collectives and lax.ppermute only.
A program may use at most 64 MiB of HBM per device.

v0:
```python
import math
import jax
import jax.numpy as jnp
from jax import lax
from jax.sharding import PartitionSpec as P


def extended(block, sides, width):
    for axis, dim in sides:
        count = lax.axis_size(axis)
        forward = [(i, i + 1) for i in range(count - 1)]
        backward = [(target, source) for source, target in forward]
        low = lax.ppermute(
            lax.slice_in_dim(block, block.shape[dim] - width, None, axis=dim), axis, forward
        )
        high = lax.ppermute(lax.slice_in_dim(block, 0, width, axis=dim), axis, backward)
        block = jnp.concatenate([low, block, high], axis=dim)
    return block


def from_behind(block, axis, distance):
    devices = range(lax.axis_size(axis))
    route = [(i - distance, i) for i in devices if i - distance in devices]
    return lax.ppermute(block, axis, route)


def correlate(signal, taps):
    return lax.conv_general_dilated(
        signal[None],
        taps[:, None, :],
        (1,),
        "VALID",
        dimension_numbers=("NCH", "OIH", "NCH"),
        feature_group_count=signal.shape[0],
        precision=lax.Precision.HIGHEST,
    )[0]


def rows_of_slab(out_grad, n_seq, n_tp):
    rows, length = out_grad.shape
    piece = rows // n_seq
    split = out_grad.reshape(n_seq, piece, length)
    mine = lax.all_to_all(split, "seq", 0, 0)
    mine = jnp.transpose(mine, (1, 0, 2)).reshape(piece, n_seq * length)
    route = []
    for a in range(n_seq):
        for b in range(n_tp):
            flat = n_seq * b + a
            route.append((a * n_tp + b, flat // n_tp * n_tp + flat % n_tp))
    moved = lax.ppermute(mine, ("seq", "tp"), route)
    return lax.all_gather(moved, "tp", axis=0, tiled=True)


def shards(streams, feat_weight, long_filter, skip_gain, out_weight, out_grad):
    channels = streams.shape[1]
    length = streams.shape[2]
    taps_long = long_filter.shape[1]
    taps_short = feat_weight.shape[2]
    n_seq = lax.axis_size("seq")
    n_tp = lax.axis_size("tp")
    reach = taps_long + taps_short - 2
    slab_grad = rows_of_slab(out_grad, n_seq, n_tp)
    slab_width = slab_grad.shape[0]
    partial_grad = jnp.dot(out_weight, slab_grad, preferred_element_type=jnp.float32)
    gated_grad = lax.psum_scatter(partial_grad, "seq", scatter_dimension=1, tiled=True)
    widened = extended(streams, (("seq", 2),), reach).astype(jnp.float32)
    short_taps = feat_weight.reshape(3 * channels, taps_short)
    feats = correlate(
        widened.reshape(3 * channels, length + 2 * reach), short_taps[:, ::-1]
    ).reshape(3, channels, -1)
    query_feat, key_feat, value_feat = (feats[0], feats[1], feats[2])
    product = key_feat * value_feat
    convolved = correlate(product, long_filter[:, ::-1])
    summed = convolved + skip_gain[:, None] * product[:, taps_long - 1 :]
    query_tail = query_feat[:, taps_long - 1 :]
    gated = (query_tail[:, :length] * summed[:, :length]).astype(jnp.bfloat16)
    gated_all = lax.all_gather(gated, "seq", axis=1, tiled=True)
    partial_out = lax.dot_general(
        out_weight, gated_all, (((0,), (0,)), ((), ())), preferred_element_type=jnp.float32
    )
    group = n_tp // n_seq
    out_rows = slab_width // group
    partial_out = (
        partial_out.reshape(group, out_rows, n_seq, length)
        .transpose(0, 2, 1, 3)
        .reshape(n_tp * out_rows, length)
    )
    output_sum = lax.psum_scatter(partial_out, "tp", scatter_dimension=0, tiled=True)
    route = []
    for s in range(n_seq):
        for p in range(n_tp):
            route.append((s * n_tp + p, p % n_seq * n_tp + group * s + p // n_seq))
    mixed = lax.ppermute(output_sum.astype(jnp.bfloat16), ("seq", "tp"), route)
    scale = 1.0 / math.sqrt(length * n_seq)
    terms = lax.dot_general(
        gated_all.reshape(channels, n_seq, length),
        slab_grad.reshape(slab_width, n_seq, length),
        (((2,), (2,)), ((1,), (1,))),
        preferred_element_type=jnp.float32,
    )
    terms = lax.reduce_precision(terms * scale, exponent_bits=8, mantissa_bits=7)
    weight_grad = jnp.sum(terms, axis=0).astype(jnp.bfloat16)
    next_grad = from_behind(gated_grad[:, :reach].astype(jnp.bfloat16), "seq", -1).astype(
        jnp.float32
    )
    grad_ext = jnp.concatenate([gated_grad, next_grad], axis=1)
    conv_grad = grad_ext * query_tail
    keep = length + taps_short - 1
    prod_grad = correlate(conv_grad, long_filter) + skip_gain[:, None] * conv_grad[:, :keep]
    query_grad = grad_ext[:, :keep] * summed[:, :keep]
    key_grad = prod_grad * value_feat[:, taps_long - 1 : taps_long - 1 + keep]
    value_grad = prod_grad * key_feat[:, taps_long - 1 : taps_long - 1 + keep]
    feat_grad = jnp.stack([query_grad, key_grad, value_grad]).reshape(3 * channels, keep)
    stream_grad = correlate(feat_grad, short_taps).reshape(3, channels, length).astype(jnp.bfloat16)
    return (mixed, stream_grad, weight_grad)


def solution(mesh):
    return jax.shard_map(
        shards,
        mesh=mesh,
        in_specs=(
            P(None, "tp", "seq"),
            P(None, "tp", None),
            P("tp", None),
            P("tp"),
            P("tp", "seq"),
            P("tp", "seq"),
        ),
        out_specs=(P("tp", "seq"), P(None, "tp", "seq"), P("tp", "seq")),
        check_vma=False,
    )
```

profile of v0, /device:TPU:4, one launch (start us, length us, event | category | flops | bytes accessed | tf_op | source)
XLA Modules:
  0.0 241.9 jit_solution(13884115816914673931)
XLA Ops:
  7.2 4.4 %all-to-all-start = ((bf16[4,128,256]{2,1,0:T(8,128)(2,1)}), bf16[4,128,256]{2,1,0:T(8,128)(2,1)S(1)}, u32[]{:S(2)}, u32[]{:S(2)}) async-start(bf16[4,128,256]{2,1,0:T(8,128)(2,1)} %bitcast.78), calls=%async_computation.1 | async-start | bytes 524288 | tf_op jit(solution)/shard_map/all_to_all | solution.py:43
  11.5 1.8 fusion.35
  14.4 3.4 %collective-permute-start = (bf16[3,512,133]{1,2,0:T(8,128)(2,1)}, bf16[3,512,133]{1,2,0:T(8,128)(2,1)S(1)}, u32[]{:S(2)}, u32[]{:S(2)}) collective-permute-start(bf16[3,512,133]{1,2,0:T(8,128)(2,1)} %copy.89), channel_id=1, source_target_pairs={{0,8},{8,16},{16,24},{1,9},{9,17},{17,25},{2,10},{10,18},{18,26},{... | collective-permute-start | bytes 1225736 | tf_op jit(solution)/shard_map/ppermute | solution.py:13
  18.8 3.4 %collective-permute-start.1 = (bf16[3,512,133]{1,2,0:T(8,128)(2,1)}, bf16[3,512,133]{1,2,0:T(8,128)(2,1)S(1)}, u32[]{:S(2)}, u32[]{:S(2)}) collective-permute-start(bf16[3,512,133]{1,2,0:T(8,128)(2,1)} %copy.90), channel_id=1, source_target_pairs={{8,0},{16,8},{24,16},{9,1},{17,9},{25,17},{10,2},{18,10},{26,18},{... | collective-permute-start | bytes 1225736 | tf_op jit(solution)/shard_map/ppermute | solution.py:16
  22.3 1.9 collective-permute-start.3
  25.8 7.5 %collective-permute-done = bf16[3,512,133]{1,2,0:T(8,128)(2,1)S(1)} collective-permute-done((bf16[3,512,133]{1,2,0:T(8,128)(2,1)}, bf16[3,512,133]{1,2,0:T(8,128)(2,1)S(1)}, u32[]{:S(2)}, u32[]{:S(2)}) %collective-permute-start) | collective-permute-done | bytes 408608 | tf_op jit(solution)/shard_map/ppermute | solution.py:13
  37.5 2.6 %pad_maximum_fusion = bf16[3,512,522]{2,1,0:T(8,128)(2,1)S(1)} fusion(bf16[3,512,133]{2,1,0:T(8,128)(2,1)} %copy.61, bf16[3,512,256]{2,1,0:T(8,128)(2,1)} %param.6, bf16[3,512,133]{2,1,0:T(8,128)(2,1)} %copy.60), kind=kLoop, calls=%fused_computation.7 | loop fusion | flops 4810752 | bytes 3207168 | tf_op jit(solution)/shard_map/concatenate | solution.py:17
  40.0 2.2 copy.62
  42.3 2.7 %pad = bf16[1536,1,528]{0,2,1:T(8,128)(2,1)} pad(bf16[1536,1,522]{0,2,1:T(8,128)(2,1)} %copy.62, bf16[]{:T(256)} %constant.12), padding=0_0x0_0x0_6 | pad | bytes 3225602 | tf_op jit(solution)/shard_map/broadcast_in_dim;reshape | solution.py:29
  45.0 1.6 reshape.44
  47.3 1.7 convolution_select_fusion
  49.0 1.7 fusion.34
  52.5 1.9 copy.70
  55.5 1.9 copy.65
  59.2 2.3 reshape.75
  62.7 1.9 slice_bitcast_fusion
  64.7 21.2 %fusion.36 = f32[1,512,389]{1,0,2:T(1,128)S(1)} fusion(f32[1,528,512]{2,0,1:T(1,128)S(1)} %copy-done.9, f32[512,1,128]{0,1,2:T(1,128)S(1)} %copy-done.13), kind=kOutput, calls=%fused_computation.57 | convolution fusion | flops 305922048 | bytes 2140160 | tf_op jit(solution)/shard_map/conv_general_dilated | solution.py:28
  88.0 4.2 %fusion.37 = f32[512,1024]{0,1:T(8,128)} fusion(bf16[512,1024]{1,0:T(8,128)(2,1)S(1)} %copy-done, bf16[1024,1024]{0,1:T(8,128)(2,1)} %all-gather.5.cloned.1.call-done), kind=kOutput, calls=%fused_computation.58 | convolution fusion | flops 1073741824 | bytes 5242880 | tf_op jit(solution)/shard_map/dot_general | solution.py:64
  92.6 29.9 %all-gather.3.cloned.1.call-done = bf16[512,1024]{0,1:T(8,128)(2,1)} async-done(((bf16[512,256]{0,1:T(8,128)(2,1)}), bf16[512,1024]{0,1:T(8,128)(2,1)}) %all-gather.3.cloned.1.call-update) | async-done | bytes 1048592 | tf_op jit(solution)/shard_map/all_gather | solution.py:77
  122.5 4.4 %convolution_bitcast_fusion = f32[1024,1024]{0,1:T(8,128)} fusion(bf16[512,1024]{0,1:T(8,128)(2,1)} %all-gather.3.cloned.1.call-done, bf16[512,1024]{1,0:T(8,128)(2,1)S(1)} %copy-done), kind=kOutput, calls=%fused_computation.6 | convolution fusion | flops 1073741824 | bytes 6291456 | tf_op jit(solution)/shard_map/dot_general | solution.py:78
  126.9 6.7 %reshape.36 = f32[2,512,4,256]{1,0,3,2:T(2,128)} reshape(f32[1024,1024]{0,1:T(8,128)} %convolution_bitcast_fusion) | data formatting | bytes 8388608 | tf_op jit(solution)/shard_map/reshape | solution.py:84
  133.6 7.3 %copy.71 = f32[2,4,512,256]{3,2,1,0:T(8,128)} copy(f32[2,4,512,256]{2,0,3,1:T(2,128)} %bitcast.71) | data formatting | bytes 8388608 | tf_op jit(solution)/shard_map/transpose | solution.py:85
  142.0 18.7 %reduce-scatter.5.cloned.1.call-done = f32[512,256]{0,1:T(8,128)} async-done(((f32[512,1024]{0,1:T(8,128)}), f32[512,256]{0,1:T(8,128)}) %reduce-scatter.5.cloned.1.call-update) | async-done | bytes 524304 | tf_op jit(solution)/shard_map/reduce_scatter | solution.py:65
  161.6 3.4 %collective-permute-start.4 = (bf16[512,133]{0,1:T(8,128)(2,1)S(1)}, bf16[512,133]{0,1:T(8,128)(2,1)S(1)}, u32[]{:S(2)}, u32[]{:S(2)}) collective-permute-start(bf16[512,133]{0,1:T(8,128)(2,1)S(1)} %slice.138), channel_id=1, source_target_pairs={{8,0},{16,8},{24,16},{9,1},{17,9},{25,17},{10,2},{18,10},{26,18},{... | collective-permute-start | bytes 408584 | tf_op jit(solution)/shard_map/ppermute | solution.py:24
  165.0 4.7 %reduce-precision_reduce_fusion = bf16[512,1024]{1,0:T(8,128)(2,1)} fusion(bf16[512,4,256]{0,2,1:T(8,128)(2,1)} %bitcast.83, bf16[1024,4,256]{0,2,1:T(8,128)(2,1)} %bitcast.82), kind=kOutput, calls=%fused_computation | convolution fusion | flops 1079508992 | bytes 4194304 | tf_op jit(solution)/shard_map/dot_general | solution.py:95
  171.1 5.4 %fusion.18 = f32[1,512,262]{1,0,2:T(1,128)S(1)} fusion(f32[512,1,128]{0,1,2:T(1,128)S(1)} %copy.75, f32[1,512,389]{1,2,0:T(8,128)S(1)} %bitcast.73), kind=kOutput, calls=%fused_computation.32 | convolution fusion | flops 206045184 | bytes 1595392 | tf_op jit(solution)/shard_map/conv_general_dilated | solution.py:28
  178.1 2.4 reshape.69
  180.4 2.7 %pad.2 = f32[1536,1,264]{0,2,1:T(8,128)} pad(f32[1536,1,262]{0,2,1:T(8,128)} %reshape.69, f32[]{:T(128)} %constant.11.clone.1), padding=0_0x0_0x0_2 | pad | bytes 3231748 | tf_op jit(solution)/shard_map/broadcast_in_dim;reshape | solution.py:29
  183.2 3.2 %reshape.55 = f32[1536,1,8,33]{0,1,3,2:T(1,128)S(1)} reshape(f32[1536,1,264]{0,2,1:T(8,128)} %pad.2) | data formatting | bytes 3244032 | tf_op jit(solution)/shard_map/conv_general_dilated | solution.py:28
  189.2 23.6 %reduce-scatter.3.cloned.1.call-done = f32[512,256]{1,0:T(8,128)} async-done(((f32[4096,256]{1,0:T(8,128)}), f32[512,256]{1,0:T(8,128)}) %reduce-scatter.3.cloned.1.call-update) | async-done | bytes 524304 | tf_op jit(solution)/shard_map/reduce_scatter | solution.py:88
  213.9 1.9 collective-permute-start.2
  217.1 17.6 %collective-permute-done.2 = bf16[512,256]{1,0:T(8,128)(2,1)S(1)} collective-permute-done((bf16[512,256]{1,0:T(8,128)(2,1)S(1)}, bf16[512,256]{1,0:T(8,128)(2,1)S(1)}, u32[]{:S(2)}, u32[]{:S(2)}) %collective-permute-start.2) | collective-permute-done | bytes 262176 | tf_op jit(solution)/shard_map/ppermute | solution.py:93
  (85 shorter events, 27.6 us)
Async XLA Ops:
  7.2 80.8 %copy-start = (bf16[512,1024]{1,0:T(8,128)(2,1)S(1)}, bf16[512,1024]{1,0:T(8,128)(2,1)}, u32[]{:S(2)}) copy-start(bf16[512,1024]{1,0:T(8,128)(2,1)} %param.10) | copy-start | bytes 3145732
  7.2 15.0 %all-to-all-start = ((bf16[4,128,256]{2,1,0:T(8,128)(2,1)}), bf16[4,128,256]{2,1,0:T(8,128)(2,1)S(1)}, u32[]{:S(2)}, u32[]{:S(2)}) async-start(bf16[4,128,256]{2,1,0:T(8,128)(2,1)} %bitcast.78), calls=%async_computation.1 | async-start | bytes 524288 | tf_op jit(solution)/shard_map/all_to_all | solution.py:43
  11.5 76.5 %all-gather.5.cloned.1.call-start = ((), (), s32[]{:S(2)}) async-start(), calls=%async_computation.5 | async-start | bytes 2359296 | tf_op jit(solution)/shard_map/all_gather | solution.py:51
  13.4 10.9 %copy-start.14 = (f32[3,512,7]{1,2,0:T(8,128)S(1)}, f32[3,512,7]{1,2,0:T(8,128)}, u32[]{:S(2)}) copy-start(f32[3,512,7]{1,2,0:T(8,128)} %param.7) | copy-start | bytes 129028
  13.4 11.2 %copy-start.10 = (f32[512,128]{1,0:T(8,128)S(1)}, f32[512,128]{1,0:T(8,128)}, u32[]{:S(2)}) copy-start(f32[512,128]{1,0:T(8,128)} %param.8) | copy-start | bytes 786436
  14.4 19.0 %collective-permute-start = (bf16[3,512,133]{1,2,0:T(8,128)(2,1)}, bf16[3,512,133]{1,2,0:T(8,128)(2,1)S(1)}, u32[]{:S(2)}, u32[]{:S(2)}) collective-permute-start(bf16[3,512,133]{1,2,0:T(8,128)(2,1)} %copy.89), channel_id=1, source_target_pairs={{0,8},{8,16},{16,24},{1,9},{9,17},{17,25},{2,10},{10,18},{18,26},{... | collective-permute-start | bytes 1225736 | tf_op jit(solution)/shard_map/ppermute | solution.py:13
  18.8 16.6 %collective-permute-start.1 = (bf16[3,512,133]{1,2,0:T(8,128)(2,1)}, bf16[3,512,133]{1,2,0:T(8,128)(2,1)S(1)}, u32[]{:S(2)}, u32[]{:S(2)}) collective-permute-start(bf16[3,512,133]{1,2,0:T(8,128)(2,1)} %copy.90), channel_id=1, source_target_pairs={{8,0},{16,8},{24,16},{9,1},{17,9},{25,17},{10,2},{18,10},{26,18},{... | collective-permute-start | bytes 1225736 | tf_op jit(solution)/shard_map/ppermute | solution.py:16
  22.3 14.2 %collective-permute-start.3 = (bf16[128,1024]{0,1:T(8,128)(2,1)S(1)}, bf16[128,1024]{0,1:T(8,128)(2,1)S(1)}, u32[]{:S(2)}, u32[]{:S(2)}) collective-permute-start(bf16[128,1024]{0,1:T(8,128)(2,1)S(1)} %bitcast.79), channel_id=1, source_target_pairs={{0,0},{1,4},{2,8},{3,12},{4,16},{5,20},{6,24},{7,28},{8,1},{9,5},{... | collective-permute-start | bytes 786440 | tf_op jit(solution)/shard_map/ppermute | solution.py:50
  36.5 0.7 copy-start.12
  37.3 85.2 %all-gather.3.cloned.1.call-start = ((), (), s32[]{:S(2)}) async-start(), calls=%async_computation.3 | async-start | bytes 1310720 | tf_op jit(solution)/shard_map/all_gather | solution.py:77
  46.6 0.7 copy-start.16
  59.2 2.3 copy-start.6
  61.5 1.2 copy-start.7
  62.7 23.5 %copy-start.2 = (f32[512,516]{0,1:T(8,128)}, f32[512,516]{0,1:T(8,128)S(1)}, u32[]{:S(2)}) copy-start(f32[512,516]{0,1:T(8,128)S(1)} %slice_bitcast_fusion.2) | copy-start | bytes 3170308
  62.7 2.0 copy-start.9
  62.7 2.0 copy-start.13
  64.7 21.2 %copy-start.15 = (f32[512]{0:T(512)S(1)}, f32[512]{0:T(512)}, u32[]{:S(2)}) copy-start(f32[512]{0:T(512)} %param.9) | copy-start | bytes 6148
  86.2 0.9 copy-start.4
  87.9 72.7 %reduce-scatter.5.cloned.1.call-start = ((), (), s32[]{:S(2)}) async-start(), calls=%async_computation.6 | async-start | bytes 2621440 | tf_op jit(solution)/shard_map/reduce_scatter | solution.py:65
  92.3 120.5 %reduce-scatter.3.cloned.1.call-start = ((), (), s32[]{:S(2)}) async-start(), calls=%async_computation.4 | async-start | bytes 4718592 | tf_op jit(solution)/shard_map/reduce_scatter | solution.py:88
  140.8 1.0 copy-start.11
  161.6 8.1 %collective-permute-start.4 = (bf16[512,133]{0,1:T(8,128)(2,1)S(1)}, bf16[512,133]{0,1:T(8,128)(2,1)S(1)}, u32[]{:S(2)}, u32[]{:S(2)}) collective-permute-start(bf16[512,133]{0,1:T(8,128)(2,1)S(1)} %slice.138), channel_id=1, source_target_pairs={{8,0},{16,8},{24,16},{9,1},{17,9},{25,17},{10,2},{18,10},{26,18},{... | collective-permute-start | bytes 408584 | tf_op jit(solution)/shard_map/ppermute | solution.py:24
  165.0 4.7 %copy-start.5 = (f32[512,389]{0,1:T(8,128)S(1)}, f32[512,389]{0,1:T(8,128)}, u32[]{:S(2)}) copy-start(f32[512,389]{0,1:T(8,128)} %copy-done.4) | copy-start | bytes 2390020
  165.0 4.7 %copy-start.8 = (f32[512,256]{0,1:T(8,128)S(1)}, f32[512,256]{0,1:T(8,128)}, u32[]{:S(2)}) copy-start(f32[512,256]{0,1:T(8,128)} %reduce-scatter.5.cloned.1.call-done) | copy-start | bytes 1572868
  169.7 1.2 copy-start.3
  186.4 0.7 copy-start.17
  212.8 22.6 %copy-start.1 = (bf16[512,1024]{1,0:T(8,128)(2,1)S(1)}, bf16[512,1024]{1,0:T(8,128)(2,1)}, u32[]{:S(2)}) copy-start(bf16[512,1024]{1,0:T(8,128)(2,1)} %param.10) | copy-start | bytes 3145732
  213.9 20.7 %collective-permute-start.2 = (bf16[512,256]{1,0:T(8,128)(2,1)S(1)}, bf16[512,256]{1,0:T(8,128)(2,1)S(1)}, u32[]{:S(2)}, u32[]{:S(2)}) collective-permute-start(bf16[512,256]{1,0:T(8,128)(2,1)S(1)} %convert_element_type.21), channel_id=1, source_target_pairs={{0,0},{1,8},{2,16},{3,24},{4,1},{5,9},{6,17},{7,25},{8,2},{9,10},{... | collective-permute-start | bytes 786440 | tf_op jit(solution)/shard_map/ppermute | solution.py:93
Sparse Core Ops, SparseCore 0:
  37.4 38.2 all-gather.4
  88.1 34.3 all-gather.2
  125.4 35.1 reduce-scatter.4
  162.8 49.9 reduce-scatter.2
where the time goes:
time: 243 us; the launch traced here: 242 us
  waiting for transfers between devices  98.2 us (40%)
  local copies, waits for them, and re-layouts  60.3 us (25%)
  matrix products  43.1 us (18%)
  starting transfers between devices  18.8 us (8%)
  between operations  14.2 us (6%)
  other arithmetic  7.25 us (3%)
    all_gather x1, waiting for transfers between devices, shards(): gated_all = lax.all_gather(gated, 'seq', axis=1, tiled=True)  29.9 us
    conv_general_dilated x4, matrix products, correlate(): lax.conv_general_dilated(signal[None], taps[:, None, :], (1,), 'VALID', d...  29.8 us
    reduce_scatter x1, waiting for transfers between devices, shards(): lax.psum_scatter(partial_out, 'tp', scatter_dimension=0, tiled=True)  23.6 us
    reduce_scatter x1, waiting for transfers between devices, shards(): lax.psum_scatter(partial_grad, 'seq', scatter_dimension=1, tiled=True)  18.7 us
    ppermute x1, waiting for transfers between devices, shards(): mixed = lax.ppermute(output_sum.astype(jnp.bfloat16), ('seq', 'tp'), route)  17.6 us
    conv_general_dilated x12, local copies, waits for them, and re-layouts, correlate(): lax.conv_general_dilated(signal[None], taps[:, None, :], (1,), 'VALID', d...  13.3 us
    another operation x4, local copies, waits for them, and re-layouts, correlate(): signal[None]  9.99 us
    unnamed x39, local copies, waits for them, and re-layouts  8.37 us
  transfers between devices with their start and end apart: 10, of which 6 were waited for; matrix products, arithmetic and copies ran while one was open for 43% of the time, Pallas kernels for 0%

commit v1 on v0

--- a/solution.py
+++ b/solution.py
@@ -74,7 +74,14 @@
     summed = convolved + skip_gain[:, None] * product[:, taps_long - 1 :]
     query_tail = query_feat[:, taps_long - 1 :]
     gated = (query_tail[:, :length] * summed[:, :length]).astype(jnp.bfloat16)
-    gated_all = lax.all_gather(gated, "seq", axis=1, tiled=True)
+    ways = lax.axis_size("seq")
+    pieces = [gated]
+    for far in range(1, ways):
+        pieces.append(
+            lax.ppermute(pieces[far - 1], "seq", [(d, (d - 1) % ways) for d in range(ways)])
+        )
+    line = jnp.concatenate(pieces, axis=1)
+    gated_all = jnp.roll(line, lax.axis_index("seq") * gated.shape[1], axis=1)
     partial_out = lax.dot_general(
         out_weight, gated_all, (((0,), (0,)), ((), ())), preferred_element_type=jnp.float32
     )

time: 243 us -> 249 us (1.025)
  waiting for transfers between devices: 98.2 us -> 81.3 us
  local copies, waits for them, and re-layouts: 60.3 us -> 69.4 us
  blocking collectives: 0 us -> 8.98 us
  starting transfers between devices: 18.8 us -> 24.4 us
    all_gather x1 -> x0, waiting for transfers between devices: 29.9 us -> none  [shards(): gated_all = lax.all_gather(gated, 'seq', axis=1, tiled=True)]
    ppermute x0 -> x3, waiting for transfers between devices: none -> 19.2 us  [shards(): lax.ppermute(pieces[far - 1], 'seq', [(d, (d - 1) % ways) for d in range(...]
    reduce_scatter x1, waiting for transfers between devices: 18.7 us -> 0.02 us  [shards(): lax.psum_scatter(partial_grad, 'seq', scatter_dimension=1, tiled=True)]
    all_to_all x0 -> x1, blocking collectives: none -> 8.98 us  [rows_of_slab(): mine = lax.all_to_all(split, 'seq', 0, 0)]
    ppermute x1, waiting for transfers between devices: 0.01 us -> 8.07 us  [rows_of_slab(): moved = lax.ppermute(mine, ('seq', 'tp'), route)]
    unnamed x39 -> x47, local copies, waits for them, and re-layouts: 8.37 us -> 14.8 us
    ppermute x1, waiting for transfers between devices: 0.83 us -> 6.56 us  [extended(): lax.ppermute(lax.slice_in_dim(block, 0, width, axis=dim), axis, backward)]
    ppermute x0 -> x3, starting transfers between devices: none -> 5.34 us  [shards(): lax.ppermute(pieces[far - 1], 'seq', [(d, (d - 1) % ways) for d in range(...]
  transfers between devices with their start and end apart: 10 -> 11, of which waited for: 6 -> 8; matrix products, arithmetic and copies ran while one was open for 43% -> 44% of each run, Pallas kernels for 0% -> 0%
where the time goes in v1:
time: 249 us; the launch traced here: 248 us
  waiting for transfers between devices  81.3 us (33%)
  local copies, waits for them, and re-layouts  69.4 us (28%)
  matrix products  41.9 us (17%)
  starting transfers between devices  24.4 us (10%)
  between operations  14.2 us (6%)
  blocking collectives  8.98 us (4%)
  other arithmetic  7.46 us (3%)
    conv_general_dilated x4, matrix products, correlate(): lax.conv_general_dilated(signal[None], taps[:, None, :], (1,), 'VALID', d...  29.7 us
    reduce_scatter x1, waiting for transfers between devices, shards(): lax.psum_scatter(partial_out, 'tp', scatter_dimension=0, tiled=True)  23.5 us
    ppermute x3, waiting for transfers between devices, shards(): lax.ppermute(pieces[far - 1], 'seq', [(d, (d - 1) % ways) for d in range(...  19.2 us
    ppermute x1, waiting for transfers between devices, shards(): mixed = lax.ppermute(output_sum.astype(jnp.bfloat16), ('seq', 'tp'), route)  17.6 us
    unnamed x47, local copies, waits for them, and re-layouts  14.8 us
    conv_general_dilated x12, local copies, waits for them, and re-layouts, correlate(): lax.conv_general_dilated(signal[None], taps[:, None, :], (1,), 'VALID', d...  12.1 us
    another operation x4, local copies, waits for them, and re-layouts, correlate(): signal[None]  10 us
    all_to_all x1, blocking collectives, rows_of_slab(): mine = lax.all_to_all(split, 'seq', 0, 0)  8.98 us
  transfers between devices with their start and end apart: 11, of which 8 were waited for; matrix products, arithmetic and copies ran while one was open for 44% of the time, Pallas kernels for 0%

profile of v1, /device:TPU:4, one launch (start us, length us, event | category | flops | bytes accessed | tf_op | source)
XLA Modules:
  0.0 247.7 jit_solution(3066382628281024608)
XLA Ops:
  7.2 9.0 %all_to_all.5 = bf16[4,128,256]{2,1,0:T(8,128)(2,1)S(1)} all-to-all(bf16[4,128,256]{2,1,0:T(8,128)(2,1)} %bitcast.79), channel_id=1, replica_groups=mesh['seq'=4,'tp'=8] {'seq'}, dimensions={0} | all-to-all | bytes 524288 | tf_op jit(solution)/shard_map/all_to_all | solution.py:43
  16.4 4.0 %collective-permute-start.6 = (bf16[128,1024]{0,1:T(8,128)(2,1)S(1)}, bf16[128,1024]{0,1:T(8,128)(2,1)S(1)}, u32[]{:S(2)}, u32[]{:S(2)}) collective-permute-start(bf16[128,1024]{0,1:T(8,128)(2,1)S(1)} %bitcast.80), channel_id=1, source_target_pairs={{0,0},{1,4},{2,8},{3,12},{4,16},{5,20},{6,24},{7,28},{8,1},{9,5},{... | collective-permute-start | bytes 786440 | tf_op jit(solution)/shard_map/ppermute | solution.py:50
  20.4 8.1 %collective-permute-done.6 = bf16[128,1024]{0,1:T(8,128)(2,1)S(1)} collective-permute-done((bf16[128,1024]{0,1:T(8,128)(2,1)S(1)}, bf16[128,1024]{0,1:T(8,128)(2,1)S(1)}, u32[]{:S(2)}, u32[]{:S(2)}) %collective-permute-start.6) | collective-permute-done | bytes 262176 | tf_op jit(solution)/shard_map/ppermute | solution.py:50
  30.7 6.0 %collective-permute-start.1 = (bf16[3,512,133]{1,2,0:T(8,128)(2,1)}, bf16[3,512,133]{1,2,0:T(8,128)(2,1)S(1)}, u32[]{:S(2)}, u32[]{:S(2)}) collective-permute-start(bf16[3,512,133]{1,2,0:T(8,128)(2,1)} %copy.89), channel_id=1, source_target_pairs={{8,0},{16,8},{24,16},{9,1},{17,9},{25,17},{10,2},{18,10},{26,18},{... | collective-permute-start | bytes 1225736 | tf_op jit(solution)/shard_map/ppermute | solution.py:16
  37.0 1.9 collective-permute-start
  40.5 6.6 %collective-permute-done.1 = bf16[3,512,133]{1,2,0:T(8,128)(2,1)S(1)} collective-permute-done((bf16[3,512,133]{1,2,0:T(8,128)(2,1)}, bf16[3,512,133]{1,2,0:T(8,128)(2,1)S(1)}, u32[]{:S(2)}, u32[]{:S(2)}) %collective-permute-start.1) | collective-permute-done | bytes 408608 | tf_op jit(solution)/shard_map/ppermute | solution.py:16
  48.2 6.3 %collective-permute-done = bf16[3,512,133]{1,2,0:T(8,128)(2,1)S(1)} collective-permute-done((bf16[3,512,133]{1,2,0:T(8,128)(2,1)S(1)}, bf16[3,512,133]{1,2,0:T(8,128)(2,1)S(1)}, u32[]{:S(2)}, u32[]{:S(2)}) %collective-permute-start) | collective-permute-done | bytes 408608 | tf_op jit(solution)/shard_map/ppermute | solution.py:13
  55.6 2.6 %pad_maximum_fusion = bf16[3,512,522]{2,1,0:T(8,128)(2,1)S(1)} fusion(bf16[3,512,133]{2,1,0:T(8,128)(2,1)} %copy.60, bf16[3,512,256]{2,1,0:T(8,128)(2,1)} %param.6, bf16[3,512,133]{2,1,0:T(8,128)(2,1)} %copy.59), kind=kLoop, calls=%fused_computation.7 | loop fusion | flops 4810752 | bytes 3207168 | tf_op jit(solution)/shard_map/concatenate | solution.py:17
  58.2 2.2 copy.61
  60.5 2.7 %pad = bf16[1536,1,528]{0,2,1:T(8,128)(2,1)} pad(bf16[1536,1,522]{0,2,1:T(8,128)(2,1)} %copy.61, bf16[]{:T(256)} %constant.41), padding=0_0x0_0x0_6 | pad | bytes 3225602 | tf_op jit(solution)/shard_map/broadcast_in_dim;reshape | solution.py:29
  70.7 1.9 copy.65
  72.6 2.3 reshape.75
  74.9 1.9 copy.69
  81.4 4.2 %fusion.38 = f32[512,1024]{0,1:T(8,128)} fusion(bf16[512,1024]{1,0:T(8,128)(2,1)S(1)} %copy-done, bf16[1024,1024]{0,1:T(8,128)(2,1)} %all-gather.2.cloned.1.call-done), kind=kOutput, calls=%fused_computation.67 | convolution fusion | flops 1073741824 | bytes 5242880 | tf_op jit(solution)/shard_map/dot_general | solution.py:64
  87.3 21.1 %fusion.37 = f32[1,512,389]{1,0,2:T(1,128)S(1)} fusion(f32[1,528,512]{2,0,1:T(1,128)S(1)} %copy-done.8, f32[512,1,128]{0,1,2:T(1,128)S(1)} %copy-done.14), kind=kOutput, calls=%fused_computation.66 | convolution fusion | flops 305922048 | bytes 2140160 | tf_op jit(solution)/shard_map/conv_general_dilated | solution.py:28
  109.7 11.9 %collective-permute-done.2 = bf16[512,256]{0,1:T(8,128)(2,1)S(1)} collective-permute-done((bf16[512,256]{0,1:T(8,128)(2,1)S(1)}, bf16[512,256]{0,1:T(8,128)(2,1)S(1)}, u32[]{:S(2)}, u32[]{:S(2)}) %collective-permute-start.2) | collective-permute-done | bytes 262176 | tf_op jit(solution)/shard_map/ppermute | solution.py:81
  121.6 1.9 collective-permute-start.3
  123.5 5.3 %collective-permute-done.3 = bf16[512,256]{0,1:T(8,128)(2,1)} collective-permute-done((bf16[512,256]{0,1:T(8,128)(2,1)S(1)}, bf16[512,256]{0,1:T(8,128)(2,1)}, u32[]{:S(2)}, u32[]{:S(2)}) %collective-permute-start.3) | collective-permute-done | bytes 262176 | tf_op jit(solution)/shard_map/ppermute | solution.py:81
  128.8 3.5 %collective-permute-start.4 = (bf16[512,256]{0,1:T(8,128)(2,1)}, bf16[512,256]{0,1:T(8,128)(2,1)}, u32[]{:S(2)}, u32[]{:S(2)}) collective-permute-start(bf16[512,256]{0,1:T(8,128)(2,1)} %collective-permute-done.3), channel_id=1, source_target_pairs={{0,24},{8,0},{16,8},{24,16},{1,25},{9,1},{17,9},{25,17},{2,26},{10... | collective-permute-start | bytes 786440 | tf_op jit(solution)/shard_map/ppermute | solution.py:81
  134.7 2.0 collective-permute-done.4
  146.5 3.2 %convolution_bitcast_fusion = f32[1024,1024]{0,1:T(8,128)} fusion(bf16[512,1024]{0,1:T(8,128)(2,1)S(1)} %constant_dynamic-slice_fusion, bf16[512,1024]{1,0:T(8,128)(2,1)S(1)} %copy-done), kind=kOutput, calls=%fused_computation.6 | convolution fusion | flops 1073741824 | bytes 6291456 | tf_op jit(solution)/shard_map/dot_general | solution.py:85
  149.7 6.7 %reshape.36 = f32[2,512,4,256]{1,0,3,2:T(2,128)} reshape(f32[1024,1024]{0,1:T(8,128)} %convolution_bitcast_fusion) | data formatting | bytes 8388608 | tf_op jit(solution)/shard_map/reshape | solution.py:91
  156.4 7.2 %copy.70 = f32[2,4,512,256]{3,2,1,0:T(8,128)} copy(f32[2,4,512,256]{2,0,3,1:T(2,128)} %bitcast.71) | data formatting | bytes 8388608 | tf_op jit(solution)/shard_map/transpose | solution.py:92
  165.7 5.1 %collective-permute-start.7 = (bf16[512,133]{0,1:T(8,128)(2,1)S(1)}, bf16[512,133]{0,1:T(8,128)(2,1)S(1)}, u32[]{:S(2)}, u32[]{:S(2)}) collective-permute-start(bf16[512,133]{0,1:T(8,128)(2,1)S(1)} %slice.138), channel_id=1, source_target_pairs={{8,0},{16,8},{24,16},{9,1},{17,9},{25,17},{10,2},{18,10},{26,18},{... | collective-permute-start | bytes 408584 | tf_op jit(solution)/shard_map/ppermute | solution.py:24
  170.8 4.7 %reduce-precision_reduce_fusion = bf16[512,1024]{1,0:T(8,128)(2,1)} fusion(bf16[512,4,256]{0,2,1:T(8,128)(2,1)} %bitcast.74, bf16[1024,4,256]{0,2,1:T(8,128)(2,1)} %bitcast.83), kind=kOutput, calls=%fused_computation | convolution fusion | flops 1079508992 | bytes 4194304 | tf_op jit(solution)/shard_map/dot_general | solution.py:102
  176.9 5.4 %fusion.18 = f32[1,512,262]{1,0,2:T(1,128)S(1)} fusion(f32[512,1,128]{0,1,2:T(1,128)S(1)} %copy.74, f32[1,512,389]{1,2,0:T(8,128)S(1)} %bitcast.73), kind=kOutput, calls=%fused_computation.32 | convolution fusion | flops 206045184 | bytes 1595392 | tf_op jit(solution)/shard_map/conv_general_dilated | solution.py:28
  183.9 2.4 reshape.69
  186.2 2.7 %pad.2 = f32[1536,1,264]{0,2,1:T(8,128)} pad(f32[1536,1,262]{0,2,1:T(8,128)} %reshape.69, f32[]{:T(128)} %constant.40.clone.1), padding=0_0x0_0x0_2 | pad | bytes 3231748 | tf_op jit(solution)/shard_map/broadcast_in_dim;reshape | solution.py:29
  188.9 3.2 %reshape.55 = f32[1536,1,8,33]{0,1,3,2:T(1,128)S(1)} reshape(f32[1536,1,264]{0,2,1:T(8,128)} %pad.2) | data formatting | bytes 3244032 | tf_op jit(solution)/shard_map/conv_general_dilated | solution.py:28
  195.0 23.5 %reduce-scatter.3.cloned.1.call-done = f32[512,256]{1,0:T(8,128)} async-done(((f32[4096,256]{1,0:T(8,128)}), f32[512,256]{1,0:T(8,128)}) %reduce-scatter.3.cloned.1.call-update) | async-done | bytes 524304 | tf_op jit(solution)/shard_map/reduce_scatter | solution.py:95
  219.7 1.9 collective-permute-start.5
  222.8 17.6 %collective-permute-done.5 = bf16[512,256]{1,0:T(8,128)(2,1)S(1)} collective-permute-done((bf16[512,256]{1,0:T(8,128)(2,1)S(1)}, bf16[512,256]{1,0:T(8,128)(2,1)S(1)}, u32[]{:S(2)}, u32[]{:S(2)}) %collective-permute-start.5) | collective-permute-done | bytes 262176 | tf_op jit(solution)/shard_map/ppermute | solution.py:100
  (97 shorter events, 44.5 us)
Async XLA Ops:
  7.2 74.3 %copy-start = (bf16[512,1024]{1,0:T(8,128)(2,1)S(1)}, bf16[512,1024]{1,0:T(8,128)(2,1)}, u32[]{:S(2)}) copy-start(bf16[512,1024]{1,0:T(8,128)(2,1)} %param.10) | copy-start | bytes 3145732
  7.2 22.1 %copy-start.2 = (bf16[3,512,256]{2,1,0:T(8,128)(2,1)S(1)}, bf16[3,512,256]{2,1,0:T(8,128)(2,1)}, u32[]{:S(2)}) copy-start(bf16[3,512,256]{2,1,0:T(8,128)(2,1)} %param.6) | copy-start | bytes 2359300
  7.2 74.2 %all-gather.2.cloned.1.call-start = ((), (), s32[]{:S(2)}) async-start(), calls=%async_computation.4 | async-start | bytes 2359296 | tf_op jit(solution)/shard_map/all_gather | solution.py:51
  16.4 12.1 %collective-permute-start.6 = (bf16[128,1024]{0,1:T(8,128)(2,1)S(1)}, bf16[128,1024]{0,1:T(8,128)(2,1)S(1)}, u32[]{:S(2)}, u32[]{:S(2)}) collective-permute-start(bf16[128,1024]{0,1:T(8,128)(2,1)S(1)} %bitcast.80), channel_id=1, source_target_pairs={{0,0},{1,4},{2,8},{3,12},{4,16},{5,20},{6,24},{7,28},{8,1},{9,5},{... | collective-permute-start | bytes 786440 | tf_op jit(solution)/shard_map/ppermute | solution.py:50
  28.5 0.7 copy-start.13
  29.2 135.5 %reduce-scatter.5.cloned.1.call-start = ((), (), s32[]{:S(2)}) async-start(), calls=%async_computation.5 | async-start | bytes 2621440 | tf_op jit(solution)/shard_map/reduce_scatter | solution.py:65
  29.7 9.2 %copy-start.15 = (f32[3,512,7]{1,2,0:T(8,128)S(1)}, f32[3,512,7]{1,2,0:T(8,128)}, u32[]{:S(2)}) copy-start(f32[3,512,7]{1,2,0:T(8,128)} %param.7) | copy-start | bytes 129028
  29.7 9.6 %copy-start.10 = (f32[512,128]{1,0:T(8,128)S(1)}, f32[512,128]{1,0:T(8,128)}, u32[]{:S(2)}) copy-start(f32[512,128]{1,0:T(8,128)} %param.8) | copy-start | bytes 786436
  30.7 16.4 %collective-permute-start.1 = (bf16[3,512,133]{1,2,0:T(8,128)(2,1)}, bf16[3,512,133]{1,2,0:T(8,128)(2,1)S(1)}, u32[]{:S(2)}, u32[]{:S(2)}) collective-permute-start(bf16[3,512,133]{1,2,0:T(8,128)(2,1)} %copy.89), channel_id=1, source_target_pairs={{8,0},{16,8},{24,16},{9,1},{17,9},{25,17},{10,2},{18,10},{26,18},{... | collective-permute-start | bytes 1225736 | tf_op jit(solution)/shard_map/ppermute | solution.py:16
  37.0 17.5 %collective-permute-start = (bf16[3,512,133]{1,2,0:T(8,128)(2,1)S(1)}, bf16[3,512,133]{1,2,0:T(8,128)(2,1)S(1)}, u32[]{:S(2)}, u32[]{:S(2)}) collective-permute-start(bf16[3,512,133]{1,2,0:T(8,128)(2,1)S(1)} %copy.88), channel_id=1, source_target_pairs={{0,8},{8,16},{16,24},{1,9},{9,17},{17,25},{2,10},{10,18},{18,26},{... | collective-permute-start | bytes 1225736 | tf_op jit(solution)/shard_map/ppermute | solution.py:13
  64.8 0.7 copy-start.17
  85.7 1.5 copy-start.14
  85.7 132.8 %reduce-scatter.3.cloned.1.call-start = ((), (), s32[]{:S(2)}) async-start(), calls=%async_computation.3 | async-start | bytes 4718592 | tf_op jit(solution)/shard_map/reduce_scatter | solution.py:95
  85.7 1.6 copy-start.8
  87.3 21.4 %copy-start.3 = (f32[512,516]{0,1:T(8,128)}, f32[512,516]{0,1:T(8,128)S(1)}, u32[]{:S(2)}) copy-start(f32[512,516]{0,1:T(8,128)S(1)} %slice_bitcast_fusion.2) | copy-start | bytes 3170308
  87.3 21.1 %copy-start.16 = (f32[512]{0:T(512)S(1)}, f32[512]{0:T(512)}, u32[]{:S(2)}) copy-start(f32[512]{0:T(512)} %param.9) | copy-start | bytes 6148
  108.7 1.0 copy-start.5
  109.7 19.1 %copy-start.12 = (bf16[512,256]{0,1:T(8,128)(2,1)}, bf16[512,256]{0,1:T(8,128)(2,1)S(1)}, u32[]{:S(2)}) copy-start(bf16[512,256]{0,1:T(8,128)(2,1)S(1)} %get-tuple-element.7) | copy-start | bytes 786436
  109.7 11.9 %collective-permute-start.2 = (bf16[512,256]{0,1:T(8,128)(2,1)S(1)}, bf16[512,256]{0,1:T(8,128)(2,1)S(1)}, u32[]{:S(2)}, u32[]{:S(2)}) collective-permute-start(bf16[512,256]{0,1:T(8,128)(2,1)S(1)} %get-tuple-element.7), channel_id=1, source_target_pairs={{0,24},{8,0},{16,8},{24,16},{1,25},{9,1},{17,9},{25,17},{2,26},{10... | collective-permute-start | bytes 786440 | tf_op jit(solution)/shard_map/ppermute | solution.py:81
  121.6 7.2 %collective-permute-start.3 = (bf16[512,256]{0,1:T(8,128)(2,1)S(1)}, bf16[512,256]{0,1:T(8,128)(2,1)}, u32[]{:S(2)}, u32[]{:S(2)}) collective-permute-start(bf16[512,256]{0,1:T(8,128)(2,1)S(1)} %collective-permute-done.2), channel_id=1, source_target_pairs={{0,24},{8,0},{16,8},{24,16},{1,25},{9,1},{17,9},{25,17},{2,26},{10... | collective-permute-start | bytes 786440 | tf_op jit(solution)/shard_map/ppermute | solution.py:81
  128.8 7.9 %collective-permute-start.4 = (bf16[512,256]{0,1:T(8,128)(2,1)}, bf16[512,256]{0,1:T(8,128)(2,1)}, u32[]{:S(2)}, u32[]{:S(2)}) collective-permute-start(bf16[512,256]{0,1:T(8,128)(2,1)} %collective-permute-done.3), channel_id=1, source_target_pairs={{0,24},{8,0},{16,8},{24,16},{1,25},{9,1},{17,9},{25,17},{2,26},{10... | collective-permute-start | bytes 786440 | tf_op jit(solution)/shard_map/ppermute | solution.py:81
  145.5 1.0 copy-start.9
  163.6 0.9 copy-start.11
  165.7 9.8 %collective-permute-start.7 = (bf16[512,133]{0,1:T(8,128)(2,1)S(1)}, bf16[512,133]{0,1:T(8,128)(2,1)S(1)}, u32[]{:S(2)}, u32[]{:S(2)}) collective-permute-start(bf16[512,133]{0,1:T(8,128)(2,1)S(1)} %slice.138), channel_id=1, source_target_pairs={{8,0},{16,8},{24,16},{9,1},{17,9},{25,17},{10,2},{18,10},{26,18},{... | collective-permute-start | bytes 408584 | tf_op jit(solution)/shard_map/ppermute | solution.py:24
  170.8 4.7 %copy-start.6 = (f32[512,389]{0,1:T(8,128)S(1)}, f32[512,389]{0,1:T(8,128)}, u32[]{:S(2)}) copy-start(f32[512,389]{0,1:T(8,128)} %copy-done.5) | copy-start | bytes 2390020
  170.8 4.7 %copy-start.7 = (f32[512,256]{0,1:T(8,128)S(1)}, f32[512,256]{0,1:T(8,128)}, u32[]{:S(2)}) copy-start(f32[512,256]{0,1:T(8,128)} %reduce-scatter.5.cloned.1.call-done) | copy-start | bytes 1572868
  175.5 1.2 copy-start.4
  192.2 0.7 copy-start.18
  218.5 22.6 %copy-start.1 = (bf16[512,1024]{1,0:T(8,128)(2,1)S(1)}, bf16[512,1024]{1,0:T(8,128)(2,1)}, u32[]{:S(2)}) copy-start(bf16[512,1024]{1,0:T(8,128)(2,1)} %param.10) | copy-start | bytes 3145732
  219.7 20.8 %collective-permute-start.5 = (bf16[512,256]{1,0:T(8,128)(2,1)S(1)}, bf16[512,256]{1,0:T(8,128)(2,1)S(1)}, u32[]{:S(2)}, u32[]{:S(2)}) collective-permute-start(bf16[512,256]{1,0:T(8,128)(2,1)S(1)} %convert_element_type.21), channel_id=1, source_target_pairs={{0,0},{1,8},{2,16},{3,24},{4,1},{5,9},{6,17},{7,25},{8,2},{9,10},{... | collective-permute-start | bytes 786440 | tf_op jit(solution)/shard_map/ppermute | solution.py:100
Sparse Core Ops, SparseCore 0:
  29.4 32.7 all-gather.1
  85.8 37.1 reduce-scatter.4
  163.7 54.7 reduce-scatter.2
